TPU v7x, 512 devices: a whole 4x8x8 slice. The times are simulated.
512 devices in a mesh: row: 32 (over z_hi, x, core), col: 16 (over z_lo, y).
Axes of the slice: x: 4, y: 8, z: 8 (z_hi: 4, z_lo: 2; z = z_hi * 2 + z_lo), core: 2. Of those that a mesh axis runs over, the one named last changes fastest.
Arguments:
- amps: float32 [32, 4, 576, 576], P(None, None, 'row', 'col'), may hold values from -6 to 6
- integrals: float32 [4, 576, 32, 576], P(None, 'row', 'col'), may hold values from -0.5 to 0.5
- e_occ: float32 [32], replicated, may hold values from -2 to -0.5
- e_vir: float32 [576], replicated, may hold values from 0.5 to 3
Outputs:
- update: float32 [32, 32, 576, 576], P('row', 'col')
All inputs are finite; a program needn't handle non-finite values.
Results may differ from a plain program's by a relative error of at most 0.00007.
Values sent between devices are 32-bit elements; how exact they have to be, the bound alone decides.
No kernel may reach another device: no remote copies, remote signals or barrier semaphores. Data moves between devices by JAX's collectives and lax.ppermute only.
A program may use at most 128 MiB of HBM per device.

v0:
```python
import jax
import jax.numpy as jnp
from jax import lax
from jax.sharding import PartitionSpec as P


def contract(left, right):
    return jnp.einsum(
        "ikac,kcjb->ijab",
        left,
        right,
        precision=lax.Precision.HIGHEST,
        preferred_element_type=jnp.float32,
    )


def shards(amps, integrals, e_occ, e_vir):
    row_count = lax.axis_size("row")
    col_count = lax.axis_size("col")
    row_index = lax.axis_index("row")
    col_index = lax.axis_index("col")
    occ_col = e_occ.shape[0] // col_count
    vir_row = e_vir.shape[0] // row_count
    a_energy = lax.dynamic_slice_in_dim(e_vir, row_index * vir_row, vir_row)
    j_energy = lax.dynamic_slice_in_dim(e_occ, col_index * occ_col, occ_col)
    gathered = lax.all_gather(integrals, "row", axis=1, tiled=True)
    contracted = contract(lax.all_gather(amps, "col", axis=3, tiled=True), gathered)
    denom = (
        e_occ[:, None, None, None]
        + j_energy[None, :, None, None]
        - a_energy[None, None, :, None]
        - e_vir[None, None, None, :]
    )
    scaled = contracted / denom
    scaled = lax.all_to_all(scaled, "row", split_axis=0, concat_axis=2, tiled=True)
    return scaled


def solution(mesh):
    placed = (P(None, None, "row", "col"), P(None, "row", "col", None), P(), P())
    return jax.shard_map(
        shards, mesh=mesh, in_specs=placed, out_specs=P("row", "col", None, None), check_vma=False
    )
```

profile of v0, /device:TPU:1, one launch (start us, length us, event | category | flops | bytes accessed | tf_op | source)
XLA Modules:
  0.0 468.0 jit_solution(11950487437803002496)
XLA Ops:
  6.5 0.0 copy-start
  6.5 0.0 copy-start.2
  6.5 0.0 copy-start.1
  6.5 0.0 all-gather.5.cloned.1.call-start
  6.5 2.6 copy.19
  9.2 0.0 all-gather.5.cloned.1.call-update
  9.2 0.0 all-gather.3.cloned.1.call-start
  9.3 0.0 copy-done
  9.3 0.8 copy.18
  10.1 0.0 all-gather.3.cloned.1.call-update
  10.1 0.0 copy-done.2
  10.1 0.1 dynamic_slice.7
  10.2 0.0 copy-done.1
  10.2 0.1 dynamic_slice.6
  10.3 0.1 broadcast_add_fusion
  10.4 0.1 broadcast_subtract_fusion
  10.4 237.1 %all-gather.5.cloned.1.call-done = f32[32,4,18,576]{0,1,2,3:T(4,128)} async-done(((f32[32,4,18,36]{0,1,2,3:T(4,128)}), f32[32,4,18,576]{0,1,2,3:T(4,128)}) %all-gather.5.cloned.1.call-update) | async-done | bytes 5308432 | tf_op jit(solution)/shard_map/all_gather | solution.py:27
  247.5 18.0 %copy.21 = f32[32,4,18,576]{3,0,1,2:T(8,128)} copy(f32[32,4,18,576]{0,1,2,3:T(4,128)} %all-gather.5.cloned.1.call-done) | data formatting | bytes 10616832 | tf_op jit(solution)/shard_map/all_gather | solution.py:27
  265.5 84.8 %all-gather.3.cloned.1.call-done = f32[4,576,2,576]{3,0,2,1:T(4,128)} async-done(((f32[4,18,2,576]{3,0,2,1:T(4,128)}), f32[4,576,2,576]{3,0,2,1:T(4,128)}) %all-gather.3.cloned.1.call-update) | async-done | bytes 10616848 | tf_op jit(solution)/shard_map/all_gather | solution.py:26
  350.2 31.1 %bitcast_divide_fusion = f32[32,2,18,576]{3,0,2,1:T(8,128)S(1)} fusion(f32[32,4,18,576]{3,0,1,2:T(8,128)} %copy.21, f32[4,576,2,576,1]{3,0,2,1,4:T(4,128)} %bitcast.17, f32[576]{0:T(1024)S(1)} %copy-done.2, f32[32,2,18]{0,2,1:T(8,128)S(1)} %broadcast_subtract_fusion), kind=kOutput, calls=%fused_computation.3 | convolution fusion | flops 18347212800 | bytes 18586368 | tf_op jit(solution)/shard_map/ikac,kcjb->ijab/dot_general | solution.py:8
  381.4 2.3 copy.22
  383.7 75.7 %all_to_all.18 = f32[32,2,18,576]{3,1,2,0:T(2,128)S(1)} all-to-all(f32[32,2,18,576]{3,1,2,0:T(2,128)S(1)} %copy.22), channel_id=1, replica_groups=mesh['row'=32,'col'=16] {'row'}, dimensions={0} | all-to-all | bytes 5308416 | tf_op jit(solution)/shard_map/all_to_all | solution.py:35
  459.3 1.8 copy.23
Async XLA Ops:
  6.5 2.7 copy-start
  6.5 3.6 copy-start.2
  6.5 3.7 copy-start.1
  6.5 241.0 %all-gather.5.cloned.1.call-start = ((), (), s32[]{:S(2)}) async-start(), calls=%async_computation.2 | async-start | bytes 22560768 | tf_op jit(solution)/shard_map/all_gather | solution.py:27
  9.2 341.0 %all-gather.3.cloned.1.call-start = ((), (), s32[]{:S(2)}) async-start(), calls=%async_computation.1 | async-start | bytes 12165120 | tf_op jit(solution)/shard_map/all_gather | solution.py:26
Sparse Core Ops, SparseCore 0:
  9.4 238.0 all-gather.4
  250.6 99.5 all-gather.2
where the time goes:
time: 469 us; the launch traced here: 468 us
  waiting for transfers between devices  322 us (69%)
  blocking collectives  75.7 us (16%)
  matrix products  31.1 us (7%)
  local copies, waits for them, and re-layouts  25.7 us (5%)
  between operations  13.4 us (3%)
    all_gather x1, waiting for transfers between devices, shards(): lax.all_gather(amps, 'col', axis=3, tiled=True)  237 us
    all_gather x1, waiting for transfers between devices, shards(): gathered = lax.all_gather(integrals, 'row', axis=1, tiled=True)  84.8 us
    all_to_all x1, blocking collectives, shards(): lax.all_to_all(scaled, 'row', split_axis=0, concat_axis=2, tiled=True)  75.7 us
    dot_general x1, matrix products, contract(): jnp.einsum('ikac,kcjb->ijab', left, right, precision=lax.Precision.HIGHES...  31.1 us
    all_gather x1, local copies, waits for them, and re-layouts, shards(): lax.all_gather(amps, 'col', axis=3, tiled=True)  18 us
  transfers between devices with their start and end apart: 2, of which 2 were waited for; matrix products, arithmetic and copies ran while one was open for 4% of the time, Pallas kernels for 0%

commit v1 on v0

v1 whole, which is shorter than its diff:
```python
import jax
import jax.numpy as jnp
from jax import lax
from jax.sharding import Mesh, PartitionSpec as P

ROWS = ("chip", "core")


def contract(left, right):
    return jnp.einsum(
        "ikac,kcjb->ijab",
        left,
        right,
        precision=lax.Precision.HIGHEST,
        preferred_element_type=jnp.float32,
    )


def shards(amps, integrals, e_occ, e_vir):
    n_chip = lax.axis_size("chip")
    n_core = lax.axis_size("core")
    chip = lax.axis_index("chip")
    core = lax.axis_index("core")
    col = lax.axis_index("col")
    occ, kw, va, vc = amps.shape
    _, vr, jc, nb = integrals.shape
    kh = kw // n_core
    ipc = occ // (n_chip * n_core) * n_core
    t = amps.reshape(n_chip, ipc, n_core, kh, va, vc).transpose(0, 2, 1, 3, 4, 5)
    t = t.reshape(n_chip * n_core, ipc, kh, va, vc)
    t = lax.all_to_all(t, ROWS, 0, 0, tiled=True)
    t = t.transpose(1, 2, 0, 3, 4).reshape(ipc, kh, -1, vc)
    t = lax.all_gather(t, "col", axis=3, tiled=True)
    g = integrals.reshape(n_core, kh, vr, jc, nb)
    g = lax.all_to_all(g, "core", 0, 0, tiled=True)
    g = g.transpose(1, 0, 2, 3, 4).reshape(kh, n_core * vr, jc, nb)
    g = lax.all_gather(g, "chip", axis=1, tiled=True)
    part = contract(t, g)
    part = lax.all_to_all(part, "core", 0, 0, tiled=True)
    contracted = part[0] + part[1]
    i_energy = lax.dynamic_slice_in_dim(e_occ, chip * n_core + core, 1)
    j_energy = lax.dynamic_slice_in_dim(e_occ, col * jc, jc)
    denom = (
        i_energy[:, None, None, None]
        + j_energy[None, :, None, None]
        - e_vir[None, None, :, None]
        - e_vir[None, None, None, :]
    )
    return contracted[None] / denom


def solution(mesh):
    rows = mesh.shape["row"]
    cols = mesh.shape["col"]
    split = Mesh(mesh.devices.reshape(rows // 2, 2, cols), ("chip", "core", "col"))
    placed = (P(None, None, ROWS, "col"), P(None, ROWS, "col", None), P(), P())
    return jax.shard_map(
        shards, mesh=split, in_specs=placed, out_specs=P(ROWS, "col", None, None), check_vma=False
    )
```

time: 469 us -> 252 us (0.54)
  waiting for transfers between devices: 322 us -> 146 us
  blocking collectives: 75.7 us -> 48.9 us
  local copies, waits for them, and re-layouts: 25.7 us -> 11.5 us
    all_gather x2, waiting for transfers between devices: 322 us -> 146 us  [the longest x1 76.8 us: shards(): t = lax.all_gather(t, 'col', axis=3, tiled=True)]
    all_to_all x1 -> x3, blocking collectives: 75.7 us -> 48.9 us  [the longest x1 21.9 us: shards(): t = lax.all_to_all(t, ROWS, 0, 0, tiled=True)]
    all_gather x1 -> x0, local copies, waits for them, and re-layouts: 18 us -> none  [shards(): lax.all_gather(amps, 'col', axis=3, tiled=True)]
where the time goes in v1:
time: 252 us
  waiting for transfers between devices  146 us (58%)
  blocking collectives  48.9 us (19%)
  matrix products  29.2 us (12%)
  between operations  13.5 us (5%)
  local copies, waits for them, and re-layouts  11.5 us (5%)
  other arithmetic  2.69 us (1%)
    all_gather x1, waiting for transfers between devices, shards(): t = lax.all_gather(t, 'col', axis=3, tiled=True)  76.8 us
    all_gather x1, waiting for transfers between devices, shards(): g = lax.all_gather(g, 'chip', axis=1, tiled=True)  69.5 us
    dot_general x1, matrix products, contract(): jnp.einsum('ikac,kcjb->ijab', left, right, precision=lax.Precision.HIGHES...  29.2 us
    all_to_all x1, blocking collectives, shards(): t = lax.all_to_all(t, ROWS, 0, 0, tiled=True)  21.9 us
    all_to_all x1, blocking collectives, shards(): part = lax.all_to_all(part, 'core', 0, 0, tiled=True)  15.5 us
    all_to_all x1, blocking collectives, shards(): g = lax.all_to_all(g, 'core', 0, 0, tiled=True)  11.6 us
  transfers between devices with their start and end apart: 2, of which 2 were waited for; matrix products, arithmetic and copies ran while one was open for 4% of the time, Pallas kernels for 0%

profile of v1, /device:TPU:1, one launch (start us, length us, event | category | flops | bytes accessed | tf_op | source)
XLA Modules:
  0.0 252.2 jit_solution(6858435136518985756)
XLA Ops:
  6.5 11.6 %all_to_all.15 = f32[2,2,18,2,576]{4,3,2,1,0:T(2,128)S(1)} all-to-all(f32[2,2,18,2,576]{4,3,2,1,0:T(2,128)} %bitcast.30), channel_id=1, replica_groups=mesh['chip'=16,'core'=2,'col'=16] {'core'}, dimensions={0} | all-to-all | bytes 663552 | tf_op jit(solution)/shard_map/all_to_all | solution.py:35
  18.2 0.8 copy.14
  19.0 0.0 all-gather.3.cloned.1.call-update
  19.0 0.0 all-gather.5.cloned.1.call-start
  19.0 1.7 copy.15
  20.7 1.8 reshape.71
  22.6 21.9 %all_to_all.16 = f32[32,1,2592]{2,1,0:T(1,128)S(1)} all-to-all(f32[32,1,2592]{2,1,0:T(1,128)S(1)} %reshape.71), channel_id=1, replica_groups=mesh['chip'=16,'core'=2,'col'=16] {'chip','core'}, dimensions={0} | all-to-all | bytes 663552 | tf_op jit(solution)/shard_map/all_to_all | solution.py:31
  44.5 0.5 broadcast.47
  45.0 1.5 reduce
  46.4 1.8 reshape.72
  48.3 0.1 bitcast_bitcast_fusion
  48.4 0.1 copy.16
  48.5 1.2 copy.17
  49.7 0.0 all-gather.5.cloned.1.call-update
  49.8 0.6 dynamic_slice.6
  50.4 0.7 dynamic-slice_add_fusion
  51.1 0.1 broadcast_subtract_fusion
  51.2 69.5 %all-gather.3.cloned.1.call-done = f32[2,576,2,576]{3,2,0,1:T(2,128)} async-done(((f32[2,36,2,576]{3,2,0,1:T(2,128)}), f32[2,576,2,576]{3,2,0,1:T(2,128)}) %all-gather.3.cloned.1.call-update) | async-done | bytes 5308432 | tf_op jit(solution)/shard_map/all_gather | solution.py:37
  120.7 76.8 %all-gather.5.cloned.1.call-done = f32[2,2,576,576]{2,1,0,3:T(2,128)} async-done(((f32[2,2,576,36]{2,1,0,3:T(2,128)}), f32[2,2,576,576]{2,1,0,3:T(2,128)}) %all-gather.5.cloned.1.call-update) | async-done | bytes 5308432 | tf_op jit(solution)/shard_map/all_gather | solution.py:33
  197.5 29.2 %fusion.5 = f32[2,2,576,576]{2,3,0,1:T(8,128)S(1)} fusion(f32[2,2,576,576]{2,1,0,3:T(2,128)} %all-gather.5.cloned.1.call-done, f32[2,576,2,576,1]{3,2,0,1,4:T(2,128)} %bitcast.31), kind=kOutput, calls=%fused_computation.6 | convolution fusion | flops 18345885696 | bytes 15925248 | tf_op jit(solution)/shard_map/ikac,kcjb->ijab/dot_general | solution.py:10
  226.7 0.4 copy.20
  227.1 15.5 %all_to_all.17 = f32[2,2,576,576]{2,3,1,0:T(8,128)S(1)} all-to-all(f32[2,2,576,576]{2,3,1,0:T(8,128)S(1)} %copy.20), channel_id=1, replica_groups=mesh['chip'=16,'core'=2,'col'=16] {'core'}, dimensions={0} | all-to-all | bytes 10616832 | tf_op jit(solution)/shard_map/all_to_all | solution.py:39
  242.6 0.5 fusion.4
  243.1 2.3 copy.21
  (6 shorter events, 0.1 us)
Async XLA Ops:
  6.5 114.2 %all-gather.3.cloned.1.call-start = ((), (), s32[]{:S(2)}) async-start(), calls=%async_computation.3 | async-start | bytes 6266880 | tf_op jit(solution)/shard_map/all_gather | solution.py:37
  19.0 178.5 %all-gather.5.cloned.1.call-start = ((), (), s32[]{:S(2)}) async-start(), calls=%async_computation.4 | async-start | bytes 6266880 | tf_op jit(solution)/shard_map/all_gather | solution.py:33
  20.7 29.0 %copy-start.1 = (f32[32]{0:T(128)S(1)}, f32[32]{0:T(128)}, u32[]{:S(2)}) copy-start(f32[32]{0:T(128)} %param.6) | copy-start | bytes 388
  20.7 30.4 %copy-start = (f32[576]{0:T(1024)S(1)}, f32[576]{0:T(1024)}, u32[]{:S(2)}) copy-start(f32[576]{0:T(1024)} %param.7) | copy-start | bytes 6916
Sparse Core Ops, SparseCore 0:
  19.1 101.5 all-gather.2
  122.8 74.6 all-gather.4

commit v2 on v1

v2 whole, which is shorter than its diff:
```python
import jax
import jax.numpy as jnp
from jax import lax
from jax.sharding import Mesh, PartitionSpec as P

CHIP = ("zh", "x")
ROWS = ("zh", "x", "core")
COLS = ("zl", "y")


def contract(left, right):
    return jnp.einsum(
        "yzikac,kzycjb->ijab",
        left,
        right,
        precision=lax.Precision.HIGHEST,
        preferred_element_type=jnp.float32,
    )


def ring_y(x):
    n = lax.axis_size("y")
    me = lax.axis_index("y")
    right = [(d, (d + 1) % n) for d in range(n)]
    left = [(d, (d - 1) % n) for d in range(n)]
    by_offset = [None] * n
    by_offset[0] = x
    from_left = from_right = x
    for step in range(1, n // 2 + 1):
        from_left = lax.ppermute(from_left, "y", right)
        by_offset[(-step) % n] = from_left
        if step < n - step:
            from_right = lax.ppermute(from_right, "y", left)
            by_offset[step] = from_right
    stacked = jnp.stack(by_offset)
    doubled = jnp.concatenate([stacked, stacked])
    return lax.dynamic_slice_in_dim(doubled, (n - me) % n, n)


def shards(amps, integrals, e_occ, e_vir):
    n_chip = lax.axis_size(CHIP)
    n_core = lax.axis_size("core")
    n_zl = lax.axis_size("zl")
    row = lax.axis_index(ROWS)
    col = lax.axis_index(COLS)
    occ, kw, va, vc = amps.shape
    _, vr, jc, nb = integrals.shape
    kh = kw // n_core
    ipc = occ // n_chip
    t = amps.reshape(n_chip, ipc, n_core, kh, va, vc).transpose(0, 2, 1, 3, 4, 5)
    t = t.reshape(n_chip * n_core, ipc, kh, va, vc)
    t = lax.all_to_all(t, ROWS, 0, 0, tiled=True)
    t = t.transpose(1, 2, 0, 3, 4).reshape(ipc, kh, -1, vc)
    other = lax.ppermute(t, "zl", [(0, 1), (1, 0)])
    first = lax.axis_index("zl") == 0
    t = jnp.stack([jnp.where(first, t, other), jnp.where(first, other, t)])
    t = ring_y(t)
    g = integrals.reshape(n_core, kh, vr, jc, nb)
    g = lax.all_to_all(g, "core", 0, 0, tiled=True)
    g = g.transpose(1, 0, 2, 3, 4).reshape(kh, n_core * vr, jc, nb)
    g = lax.all_gather(g, CHIP, axis=1, tiled=True)
    g = g.reshape(kh, n_zl, lax.axis_size("y"), vc, jc, nb)
    part = contract(t, g)
    part = lax.all_to_all(part, "core", 0, 0, tiled=True)
    contracted = part[0] + part[1]
    i_energy = lax.dynamic_slice_in_dim(e_occ, row, 1)
    j_energy = lax.dynamic_slice_in_dim(e_occ, col * jc, jc)
    denom = (
        i_energy[:, None, None, None]
        + j_energy[None, :, None, None]
        - e_vir[None, None, :, None]
        - e_vir[None, None, None, :]
    )
    return contracted[None] / denom


def solution(mesh):
    devices = mesh.devices.reshape(4, mesh.shape["row"] // 8, 2, 2, mesh.shape["col"] // 2)
    split = Mesh(devices, ("zh", "x", "core", "zl", "y"))
    placed = (P(None, None, ROWS, COLS), P(None, ROWS, COLS, None), P(), P())
    return jax.shard_map(
        shards, mesh=split, in_specs=placed, out_specs=P(ROWS, COLS, None, None), check_vma=False
    )
```

time: 252 us -> 212 us (0.84); the launches traced: 252 us -> 209 us
  waiting for transfers between devices: 146 us -> 57.7 us
  starting transfers between devices: 0.04 us -> 30.1 us
  local copies, waits for them, and re-layouts: 11.5 us -> 27.3 us
  other arithmetic: 2.69 us -> 6.29 us
  blocking collectives: 48.9 us -> 45.9 us
    all_gather x2 -> x1, waiting for transfers between devices: 146 us -> 0.01 us  [shards(): g = lax.all_gather(g, CHIP, axis=1, tiled=True)]
    ppermute x0 -> x8, waiting for transfers between devices: none -> 57.6 us  [the longest x4 48.8 us: ring_y(): from_left = lax.ppermute(from_left, 'y', right)]
    ppermute x0 -> x8, starting transfers between devices: none -> 30.1 us  [the longest x3 13.6 us: ring_y(): from_right = lax.ppermute(from_right, 'y', left)]
    unnamed x6 -> x19, local copies, waits for them, and re-layouts: 3.68 us -> 20.9 us
    all_to_all x1, blocking collectives: 15.5 us -> 12.4 us  [shards(): part = lax.all_to_all(part, 'core', 0, 0, tiled=True)]
  transfers between devices with their start and end apart: 2 -> 9, of which waited for: 2 -> 5; matrix products, arithmetic and copies ran while one was open for 4% -> 15% of each run, Pallas kernels for 0% -> 0%
where the time goes in v2:
time: 212 us; the launch traced here: 209 us
  waiting for transfers between devices  57.7 us (27%)
  blocking collectives  45.9 us (22%)
  starting transfers between devices  30.1 us (14%)
  matrix products  27.9 us (13%)
  local copies, waits for them, and re-layouts  27.3 us (13%)
  between operations  13.6 us (6%)
  other arithmetic  6.29 us (3%)
    ppermute x4, waiting for transfers between devices, ring_y(): from_left = lax.ppermute(from_left, 'y', right)  48.8 us
    dot_general x1, matrix products, contract(): jnp.einsum('yzikac,kzycjb->ijab', left, right, precision=lax.Precision.HI...  27.9 us
    all_to_all x1, blocking collectives, shards(): t = lax.all_to_all(t, ROWS, 0, 0, tiled=True)  21.8 us
    unnamed x19, local copies, waits for them, and re-layouts  20.9 us
    ppermute x3, starting transfers between devices, ring_y(): from_right = lax.ppermute(from_right, 'y', left)  13.6 us
    all_to_all x1, blocking collectives, shards(): part = lax.all_to_all(part, 'core', 0, 0, tiled=True)  12.4 us
    all_to_all x1, blocking collectives, shards(): g = lax.all_to_all(g, 'core', 0, 0, tiled=True)  11.7 us
    ppermute x4, starting transfers between devices, ring_y(): from_left = lax.ppermute(from_left, 'y', right)  9.24 us
  transfers between devices with their start and end apart: 9, of which 5 were waited for; matrix products, arithmetic and copies ran while one was open for 15% of the time, Pallas kernels for 0%

profile of v2, /device:TPU:1, one launch (start us, length us, event | category | flops | bytes accessed | tf_op | source)
XLA Modules:
  0.0 208.8 jit_solution(4651076916289586803)
XLA Ops:
  6.5 11.7 %all_to_all.15 = f32[2,2,18,2,576]{4,3,2,1,0:T(2,128)S(1)} all-to-all(f32[2,2,18,2,576]{4,3,2,1,0:T(2,128)} %bitcast.63), channel_id=1, replica_groups=mesh['zh'=4,'x'=4,'core'=2,'zl'=2,'y'=8] {'core'}, dimensions={0} | all-to-all | bytes 663552 | tf_op jit(solution)/shard_map/all_to_all | solution.py:59
  20.7 1.8 reshape.75
  22.6 21.8 %all_to_all.16 = f32[32,1,2592]{2,1,0:T(1,128)S(1)} all-to-all(f32[32,1,2592]{2,1,0:T(1,128)S(1)} %reshape.75), channel_id=1, replica_groups=mesh['zh'=4,'x'=4,'core'=2,'zl'=2,'y'=8] {'zh','x','core'}, dimensions={0} | all-to-all | bytes 663552 | tf_op jit(solution)/shard_map/all_to_all | solution.py:52
  46.4 1.8 reshape.76
  49.1 7.2 %collective-permute-start = (f32[2,2,576,36]{2,3,0,1:T(8,128)S(1)}, f32[2,2,576,36]{2,3,0,1:T(8,128)S(1)}, u32[]{:S(2)}, u32[]{:S(2)}) collective-permute-start(f32[2,2,576,36]{2,3,0,1:T(8,128)S(1)} %copy.63), channel_id=1, source_target_pairs={{0,8},{8,0},{1,9},{9,1},{2,10},{10,2},{3,11},{11,3},{4,12},{12,4},... | collective-permute-start | bytes 995336 | tf_op jit(solution)/shard_map/ppermute | solution.py:54
  56.3 8.8 %collective-permute-done = f32[2,2,576,36]{2,3,0,1:T(8,128)S(1)} collective-permute-done((f32[2,2,576,36]{2,3,0,1:T(8,128)S(1)}, f32[2,2,576,36]{2,3,0,1:T(8,128)S(1)}, u32[]{:S(2)}, u32[]{:S(2)}) %collective-permute-start) | collective-permute-done | bytes 331808 | tf_op jit(solution)/shard_map/ppermute | solution.py:54
  65.9 3.5 %collective-permute-start.4 = (f32[2,2,2,576,36]{3,2,4,1,0:T(2,128)S(1)}, f32[2,2,2,576,36]{3,2,4,1,0:T(2,128)S(1)}, u32[]{:S(2)}, u32[]{:S(2)}) collective-permute-start(f32[2,2,2,576,36]{3,2,4,1,0:T(2,128)S(1)} %copy.66), channel_id=1, source_target_pairs={{0,1},{1,2},{2,3},{3,4},{4,5},{5,6},{6,7},{7,0},{8,9},{9,10},{10,1... | collective-permute-start | bytes 1990664 | tf_op jit(solution)/shard_map/ppermute | solution.py:30
  69.4 4.5 %collective-permute-start.1 = (f32[2,2,2,576,36]{3,2,4,1,0:T(2,128)S(1)}, f32[2,2,2,576,36]{3,2,4,1,0:T(2,128)S(1)}, u32[]{:S(2)}, u32[]{:S(2)}) collective-permute-start(f32[2,2,2,576,36]{3,2,4,1,0:T(2,128)S(1)} %copy.66), channel_id=1, source_target_pairs={{0,7},{1,0},{2,1},{3,2},{4,3},{5,4},{6,5},{7,6},{8,15},{9,8},{10,9... | collective-permute-start | bytes 1990664 | tf_op jit(solution)/shard_map/ppermute | solution.py:33
  73.9 13.9 %collective-permute-done.4 = f32[2,2,2,576,36]{3,2,4,1,0:T(2,128)S(1)} collective-permute-done((f32[2,2,2,576,36]{3,2,4,1,0:T(2,128)S(1)}, f32[2,2,2,576,36]{3,2,4,1,0:T(2,128)S(1)}, u32[]{:S(2)}, u32[]{:S(2)}) %collective-permute-start.4) | collective-permute-done | bytes 663584 | tf_op jit(solution)/shard_map/ppermute | solution.py:30
  87.8 1.9 collective-permute-start.5
  89.7 4.6 %collective-permute-start.2 = (f32[2,2,2,576,36]{3,2,4,1,0:T(2,128)S(1)}, f32[2,2,2,576,36]{3,2,4,1,0:T(2,128)}, u32[]{:S(2)}, u32[]{:S(2)}) collective-permute-start(f32[2,2,2,576,36]{3,2,4,1,0:T(2,128)S(1)} %collective-permute-done.1), channel_id=1, source_target_pairs={{0,7},{1,0},{2,1},{3,2},{4,3},{5,4},{6,5},{7,6},{8,15},{9,8},{10,9... | collective-permute-start | bytes 1990664 | tf_op jit(solution)/shard_map/ppermute | solution.py:33
  94.3 13.1 %collective-permute-done.5 = f32[2,2,2,576,36]{3,2,4,1,0:T(2,128)S(1)} collective-permute-done((f32[2,2,2,576,36]{3,2,4,1,0:T(2,128)S(1)}, f32[2,2,2,576,36]{3,2,4,1,0:T(2,128)S(1)}, u32[]{:S(2)}, u32[]{:S(2)}) %collective-permute-start.5) | collective-permute-done | bytes 663584 | tf_op jit(solution)/shard_map/ppermute | solution.py:30
  107.4 1.9 collective-permute-start.6
  110.7 4.6 %collective-permute-start.3 = (f32[2,2,2,576,36]{3,2,4,1,0:T(2,128)}, f32[2,2,2,576,36]{3,2,4,1,0:T(2,128)S(1)}, u32[]{:S(2)}, u32[]{:S(2)}) collective-permute-start(f32[2,2,2,576,36]{3,2,4,1,0:T(2,128)} %collective-permute-done.2), channel_id=1, source_target_pairs={{0,7},{1,0},{2,1},{3,2},{4,3},{5,4},{6,5},{7,6},{8,15},{9,8},{10,9... | collective-permute-start | bytes 1990664 | tf_op jit(solution)/shard_map/ppermute | solution.py:33
  116.3 9.8 %collective-permute-done.6 = f32[2,2,2,576,36]{3,2,4,1,0:T(2,128)} collective-permute-done((f32[2,2,2,576,36]{3,2,4,1,0:T(2,128)S(1)}, f32[2,2,2,576,36]{3,2,4,1,0:T(2,128)}, u32[]{:S(2)}, u32[]{:S(2)}) %collective-permute-start.6) | collective-permute-done | bytes 663584 | tf_op jit(solution)/shard_map/ppermute | solution.py:30
  126.1 1.9 collective-permute-start.7
  129.0 2.1 %bitcast_dynamic-update-slice_fusion.10 = f32[16,2,2,2,576,36]{4,5,1,0,2,3:T(8,128)} fusion(f32[16,2,2,2,576,36]{4,5,1,0,2,3:T(8,128)} %bitcast_dynamic-update-slice_fusion.12, f32[2,2,2,576,36]{3,2,4,1,0:T(2,128)} %collective-permute-done.2), kind=kLoop, calls=%fused_computation.18 | loop fusion | bytes 1556480
  132.1 12.0 %collective-permute-done.7 = f32[2,2,2,576,36]{3,2,4,1,0:T(2,128)S(1)} collective-permute-done((f32[2,2,2,576,36]{3,2,4,1,0:T(2,128)}, f32[2,2,2,576,36]{3,2,4,1,0:T(2,128)S(1)}, u32[]{:S(2)}, u32[]{:S(2)}) %collective-permute-start.7) | collective-permute-done | bytes 663584 | tf_op jit(solution)/shard_map/ppermute | solution.py:30
  145.0 2.1 bitcast_dynamic-update-slice_fusion.4
  151.0 2.1 %bitcast_dynamic-update-slice_fusion.11 = f32[16,2,2,2,576,36]{4,5,1,0,2,3:T(8,128)} fusion(f32[16,2,2,2,576,36]{4,5,1,0,2,3:T(8,128)} %bitcast_dynamic-update-slice_fusion.13, f32[2,2,2,576,36]{3,2,4,1,0:T(2,128)} %collective-permute-done.2), kind=kLoop, calls=%fused_computation.19 | loop fusion | bytes 1556480
  155.1 2.1 %bitcast_dynamic-update-slice_fusion.5 = f32[16,2,2,2,576,36]{4,5,1,0,2,3:T(8,128)} fusion(f32[16,2,2,2,576,36]{4,5,1,0,2,3:T(8,128)} %bitcast_dynamic-update-slice_fusion.7, f32[2,2,2,576,36]{3,2,4,1,0:T(2,128)} %collective-permute-done.6), kind=kLoop, calls=%fused_computation.13 | loop fusion | bytes 1556480
  159.2 27.9 %fusion = f32[2,576,2,576,1,1,1]{3,1,6,5,0,2,4:T(8,128)S(1)} fusion(f32[2,2,8,36,2,576,1]{5,4,3,2,1,0,6:T(2,128)} %bitcast.64, f32[16,2,2,2,576,36]{4,5,1,0,2,3:T(8,128)} %bitcast_dynamic-update-slice_fusion.1, s32[]{:T(128)S(6)} %select_n.32), kind=kOutput, calls=%fused_computation | convolution fusion | flops 18345885696 | bytes 17760260 | tf_op jit(solution)/shard_map/yzikac,kzycjb->ijab/dot_general | solution.py:12
  187.5 12.4 %all_to_all.17 = f32[2,2,576,576]{3,2,1,0:T(8,128)S(1)} all-to-all(f32[2,2,576,576]{3,2,1,0:T(8,128)S(1)} %bitcast.57), channel_id=1, replica_groups=mesh['zh'=4,'x'=4,'core'=2,'zl'=2,'y'=8] {'core'}, dimensions={0} | all-to-all | bytes 10616832 | tf_op jit(solution)/shard_map/all_to_all | solution.py:64
  199.9 2.1 fusion.4
  (36 shorter events, 19.5 us)
Async XLA Ops:
  6.5 102.8 %copy-start.1 = (f32[32]{0:T(128)S(1)}, f32[32]{0:T(128)}, u32[]{:S(2)}) copy-start(f32[32]{0:T(128)} %param.6) | copy-start | bytes 388
  6.5 104.1 %copy-start = (f32[576]{0:T(1024)S(1)}, f32[576]{0:T(1024)}, u32[]{:S(2)}) copy-start(f32[576]{0:T(1024)} %param.7) | copy-start | bytes 6916
  6.5 152.6 %all-gather.2.cloned.1.call-start = ((), (), s32[]{:S(2)}) async-start(), calls=%async_computation.3 | async-start | bytes 6266880 | tf_op jit(solution)/shard_map/all_gather | solution.py:61
  49.1 16.1 %collective-permute-start = (f32[2,2,576,36]{2,3,0,1:T(8,128)S(1)}, f32[2,2,576,36]{2,3,0,1:T(8,128)S(1)}, u32[]{:S(2)}, u32[]{:S(2)}) collective-permute-start(f32[2,2,576,36]{2,3,0,1:T(8,128)S(1)} %copy.63), channel_id=1, source_target_pairs={{0,8},{8,0},{1,9},{9,1},{2,10},{10,2},{3,11},{11,3},{4,12},{12,4},... | collective-permute-start | bytes 995336 | tf_op jit(solution)/shard_map/ppermute | solution.py:54
  65.9 21.9 %collective-permute-start.4 = (f32[2,2,2,576,36]{3,2,4,1,0:T(2,128)S(1)}, f32[2,2,2,576,36]{3,2,4,1,0:T(2,128)S(1)}, u32[]{:S(2)}, u32[]{:S(2)}) collective-permute-start(f32[2,2,2,576,36]{3,2,4,1,0:T(2,128)S(1)} %copy.66), channel_id=1, source_target_pairs={{0,1},{1,2},{2,3},{3,4},{4,5},{5,6},{6,7},{7,0},{8,9},{9,10},{10,1... | collective-permute-start | bytes 1990664 | tf_op jit(solution)/shard_map/ppermute | solution.py:30
  69.4 20.3 %collective-permute-start.1 = (f32[2,2,2,576,36]{3,2,4,1,0:T(2,128)S(1)}, f32[2,2,2,576,36]{3,2,4,1,0:T(2,128)S(1)}, u32[]{:S(2)}, u32[]{:S(2)}) collective-permute-start(f32[2,2,2,576,36]{3,2,4,1,0:T(2,128)S(1)} %copy.66), channel_id=1, source_target_pairs={{0,7},{1,0},{2,1},{3,2},{4,3},{5,4},{6,5},{7,6},{8,15},{9,8},{10,9... | collective-permute-start | bytes 1990664 | tf_op jit(solution)/shard_map/ppermute | solution.py:33
  87.8 19.6 %collective-permute-start.5 = (f32[2,2,2,576,36]{3,2,4,1,0:T(2,128)S(1)}, f32[2,2,2,576,36]{3,2,4,1,0:T(2,128)S(1)}, u32[]{:S(2)}, u32[]{:S(2)}) collective-permute-start(f32[2,2,2,576,36]{3,2,4,1,0:T(2,128)S(1)} %collective-permute-done.4), channel_id=1, source_target_pairs={{0,1},{1,2},{2,3},{3,4},{4,5},{5,6},{6,7},{7,0},{8,9},{9,10},{10,1... | collective-permute-start | bytes 1990664 | tf_op jit(solution)/shard_map/ppermute | solution.py:30
  89.7 21.0 %collective-permute-start.2 = (f32[2,2,2,576,36]{3,2,4,1,0:T(2,128)S(1)}, f32[2,2,2,576,36]{3,2,4,1,0:T(2,128)}, u32[]{:S(2)}, u32[]{:S(2)}) collective-permute-start(f32[2,2,2,576,36]{3,2,4,1,0:T(2,128)S(1)} %collective-permute-done.1), channel_id=1, source_target_pairs={{0,7},{1,0},{2,1},{3,2},{4,3},{5,4},{6,5},{7,6},{8,15},{9,8},{10,9... | collective-permute-start | bytes 1990664 | tf_op jit(solution)/shard_map/ppermute | solution.py:33
  107.4 18.8 %collective-permute-start.6 = (f32[2,2,2,576,36]{3,2,4,1,0:T(2,128)S(1)}, f32[2,2,2,576,36]{3,2,4,1,0:T(2,128)}, u32[]{:S(2)}, u32[]{:S(2)}) collective-permute-start(f32[2,2,2,576,36]{3,2,4,1,0:T(2,128)S(1)} %collective-permute-done.5), channel_id=1, source_target_pairs={{0,1},{1,2},{2,3},{3,4},{4,5},{5,6},{6,7},{7,0},{8,9},{9,10},{10,1... | collective-permute-start | bytes 1990664 | tf_op jit(solution)/shard_map/ppermute | solution.py:30
  110.7 20.4 %collective-permute-start.3 = (f32[2,2,2,576,36]{3,2,4,1,0:T(2,128)}, f32[2,2,2,576,36]{3,2,4,1,0:T(2,128)S(1)}, u32[]{:S(2)}, u32[]{:S(2)}) collective-permute-start(f32[2,2,2,576,36]{3,2,4,1,0:T(2,128)} %collective-permute-done.2), channel_id=1, source_target_pairs={{0,7},{1,0},{2,1},{3,2},{4,3},{5,4},{6,5},{7,6},{8,15},{9,8},{10,9... | collective-permute-start | bytes 1990664 | tf_op jit(solution)/shard_map/ppermute | solution.py:33
  126.1 17.9 %collective-permute-start.7 = (f32[2,2,2,576,36]{3,2,4,1,0:T(2,128)}, f32[2,2,2,576,36]{3,2,4,1,0:T(2,128)S(1)}, u32[]{:S(2)}, u32[]{:S(2)}) collective-permute-start(f32[2,2,2,576,36]{3,2,4,1,0:T(2,128)} %collective-permute-done.6), channel_id=1, source_target_pairs={{0,1},{1,2},{2,3},{3,4},{4,5},{5,6},{6,7},{7,0},{8,9},{9,10},{10,1... | collective-permute-start | bytes 1990664 | tf_op jit(solution)/shard_map/ppermute | solution.py:30
Sparse Core Ops, SparseCore 0:
  19.2 101.8 all-gather.1

commit v3 on v2

--- a/solution.py
+++ b/solution.py
@@ -13,7 +13,7 @@
         "yzikac,kzycjb->ijab",
         left,
         right,
-        precision=lax.Precision.HIGHEST,
+        precision=lax.Precision.HIGH,
         preferred_element_type=jnp.float32,
     )
 
@@ -32,9 +32,7 @@
         if step < n - step:
             from_right = lax.ppermute(from_right, "y", left)
             by_offset[step] = from_right
-    stacked = jnp.stack(by_offset)
-    doubled = jnp.concatenate([stacked, stacked])
-    return lax.dynamic_slice_in_dim(doubled, (n - me) % n, n)
+    return jnp.stack(by_offset)
 
 
 def shards(amps, integrals, e_occ, e_vir):
@@ -51,6 +49,7 @@
     t = t.reshape(n_chip * n_core, ipc, kh, va, vc)
     t = lax.all_to_all(t, ROWS, 0, 0, tiled=True)
     t = t.transpose(1, 2, 0, 3, 4).reshape(ipc, kh, -1, vc)
+    t, integrals = lax.optimization_barrier((t, integrals))
     other = lax.ppermute(t, "zl", [(0, 1), (1, 0)])
     first = lax.axis_index("zl") == 0
     t = jnp.stack([jnp.where(first, t, other), jnp.where(first, other, t)])
@@ -59,7 +58,10 @@
     g = lax.all_to_all(g, "core", 0, 0, tiled=True)
     g = g.transpose(1, 0, 2, 3, 4).reshape(kh, n_core * vr, jc, nb)
     g = lax.all_gather(g, CHIP, axis=1, tiled=True)
-    g = g.reshape(kh, n_zl, lax.axis_size("y"), vc, jc, nb)
+    n_y = lax.axis_size("y")
+    g = g.reshape(kh, n_zl, n_y, vc, jc, nb)
+    g = jnp.concatenate([g, g], axis=2)
+    g = lax.dynamic_slice_in_dim(g, lax.axis_index("y"), n_y, axis=2)
     part = contract(t, g)
     part = lax.all_to_all(part, "core", 0, 0, tiled=True)
     contracted = part[0] + part[1]

time: 212 us -> 187 us (0.88)
  matrix products: 27.9 us -> 18.3 us
  blocking collectives: 45.9 us -> 41.3 us
  starting transfers between devices: 30.1 us -> 25.6 us
  local copies, waits for them, and re-layouts: 27.3 us -> 23.7 us
  other arithmetic: 6.29 us -> 3.79 us
    dot_general x1, matrix products: 27.9 us -> 18.3 us  [contract(): jnp.einsum('yzikac,kzycjb->ijab', left, right, precision=lax.Precision.HI...]
    unnamed x19 -> x14, local copies, waits for them, and re-layouts: 20.9 us -> 11.7 us
    all_to_all x1, blocking collectives: 11.7 us -> 3.66 us  [shards(): g = lax.all_to_all(g, 'core', 0, 0, tiled=True)]
    all_to_all x1, blocking collectives: 21.8 us -> 28.7 us  [shards(): t = lax.all_to_all(t, ROWS, 0, 0, tiled=True)]
    ppermute x4, waiting for transfers between devices: 48.8 us -> 43.2 us  [ring_y(): from_left = lax.ppermute(from_left, 'y', right)]
    all_gather x1, waiting for transfers between devices: 0.01 us -> 4.71 us  [shards(): g = lax.all_gather(g, CHIP, axis=1, tiled=True)]
    ppermute x1, starting transfers between devices: 7.24 us -> 3.51 us  [shards(): other = lax.ppermute(t, 'zl', [(0, 1), (1, 0)])]
    all_to_all x1, blocking collectives: 12.4 us -> 8.95 us  [shards(): part = lax.all_to_all(part, 'core', 0, 0, tiled=True)]
  transfers between devices with their start and end apart: 9 -> 9, of which waited for: 5 -> 6; matrix products, arithmetic and copies ran while one was open for 15% -> 7% of each run, Pallas kernels for 0% -> 0%
where the time goes in v3:
time: 187 us; the launch traced here: 184 us
  waiting for transfers between devices  57.3 us (31%)
  blocking collectives  41.3 us (22%)
  starting transfers between devices  25.6 us (14%)
  local copies, waits for them, and re-layouts  23.7 us (13%)
  matrix products  18.3 us (10%)
  between operations  13.6 us (7%)
  other arithmetic  3.79 us (2%)
    ppermute x4, waiting for transfers between devices, ring_y(): from_left = lax.ppermute(from_left, 'y', right)  43.2 us
    all_to_all x1, blocking collectives, shards(): t = lax.all_to_all(t, ROWS, 0, 0, tiled=True)  28.7 us
    dot_general x1, matrix products, contract(): jnp.einsum('yzikac,kzycjb->ijab', left, right, precision=lax.Precision.HI...  18.3 us
    ppermute x3, starting transfers between devices, ring_y(): from_right = lax.ppermute(from_right, 'y', left)  12.9 us
    unnamed x14, local copies, waits for them, and re-layouts  11.7 us
    ppermute x1, waiting for transfers between devices, shards(): other = lax.ppermute(t, 'zl', [(0, 1), (1, 0)])  9.37 us
    ppermute x4, starting transfers between devices, ring_y(): from_left = lax.ppermute(from_left, 'y', right)  9.11 us
    all_to_all x1, blocking collectives, shards(): part = lax.all_to_all(part, 'core', 0, 0, tiled=True)  8.95 us
  transfers between devices with their start and end apart: 9, of which 6 were waited for; matrix products, arithmetic and copies ran while one was open for 7% of the time, Pallas kernels for 0%

profile of v3, /device:TPU:1, one launch (start us, length us, event | category | flops | bytes accessed | tf_op | source)
XLA Modules:
  0.0 183.6 jit_solution(5846470159349495211)
XLA Ops:
  8.3 1.8 reshape.75
  10.1 28.7 %all_to_all.15 = f32[32,1,2592]{2,1,0:T(1,128)S(1)} all-to-all(f32[32,1,2592]{2,1,0:T(1,128)S(1)} %reshape.75), channel_id=1, replica_groups=mesh['zh'=4,'x'=4,'core'=2,'zl'=2,'y'=8] {'zh','x','core'}, dimensions={0} | all-to-all | bytes 663552 | tf_op jit(solution)/shard_map/all_to_all | solution.py:50
  40.8 1.8 reshape.76
  42.9 3.7 %all_to_all.16 = f32[2,2,18,2,576]{4,3,2,1,0:T(2,128)S(1)} all-to-all(f32[2,2,18,2,576]{4,3,2,1,0:T(2,128)S(1)} %bitcast.59), channel_id=1, replica_groups=mesh['zh'=4,'x'=4,'core'=2,'zl'=2,'y'=8] {'core'}, dimensions={0} | all-to-all | bytes 663552 | tf_op jit(solution)/shard_map/all_to_all | solution.py:58
  47.9 3.5 %collective-permute-start = (f32[2,2,576,36]{2,3,0,1:T(8,128)S(1)}, f32[2,2,576,36]{2,3,0,1:T(8,128)S(1)}, u32[]{:S(2)}, u32[]{:S(2)}) collective-permute-start(f32[2,2,576,36]{2,3,0,1:T(8,128)S(1)} %copy.37), channel_id=1, source_target_pairs={{0,8},{8,0},{1,9},{9,1},{2,10},{10,2},{3,11},{11,3},{4,12},{12,4},... | collective-permute-start | bytes 995336 | tf_op jit(solution)/shard_map/ppermute | solution.py:53
  51.5 9.4 %collective-permute-done = f32[2,2,576,36]{2,3,0,1:T(8,128)S(1)} collective-permute-done((f32[2,2,576,36]{2,3,0,1:T(8,128)S(1)}, f32[2,2,576,36]{2,3,0,1:T(8,128)S(1)}, u32[]{:S(2)}, u32[]{:S(2)}) %collective-permute-start) | collective-permute-done | bytes 331808 | tf_op jit(solution)/shard_map/ppermute | solution.py:53
  61.5 3.2 %collective-permute-start.4 = (f32[2,2,2,576,36]{3,2,4,1,0:T(2,128)S(1)}, f32[2,2,2,576,36]{3,2,4,1,0:T(2,128)S(1)}, u32[]{:S(2)}, u32[]{:S(2)}) collective-permute-start(f32[2,2,2,576,36]{3,2,4,1,0:T(2,128)S(1)} %copy.40), channel_id=1, source_target_pairs={{0,1},{1,2},{2,3},{3,4},{4,5},{5,6},{6,7},{7,0},{8,9},{9,10},{10,1... | collective-permute-start | bytes 1990664 | tf_op jit(solution)/shard_map/ppermute | solution.py:30
  64.7 3.8 %collective-permute-start.1 = (f32[2,2,2,576,36]{3,2,4,1,0:T(2,128)S(1)}, f32[2,2,2,576,36]{3,2,4,1,0:T(2,128)S(1)}, u32[]{:S(2)}, u32[]{:S(2)}) collective-permute-start(f32[2,2,2,576,36]{3,2,4,1,0:T(2,128)S(1)} %copy.40), channel_id=1, source_target_pairs={{0,7},{1,0},{2,1},{3,2},{4,3},{5,4},{6,5},{7,6},{8,15},{9,8},{10,9... | collective-permute-start | bytes 1990664 | tf_op jit(solution)/shard_map/ppermute | solution.py:33
  68.6 12.5 %collective-permute-done.4 = f32[2,2,2,576,36]{3,2,4,1,0:T(2,128)S(1)} collective-permute-done((f32[2,2,2,576,36]{3,2,4,1,0:T(2,128)S(1)}, f32[2,2,2,576,36]{3,2,4,1,0:T(2,128)S(1)}, u32[]{:S(2)}, u32[]{:S(2)}) %collective-permute-start.4) | collective-permute-done | bytes 663584 | tf_op jit(solution)/shard_map/ppermute | solution.py:30
  81.1 1.9 %collective-permute-start.5 = (f32[2,2,2,576,36]{3,2,4,1,0:T(2,128)S(1)}, f32[2,2,2,576,36]{3,2,4,1,0:T(2,128)S(1)}, u32[]{:S(2)}, u32[]{:S(2)}) collective-permute-start(f32[2,2,2,576,36]{3,2,4,1,0:T(2,128)S(1)} %collective-permute-done.4), channel_id=1, source_target_pairs={{0,1},{1,2},{2,3},{3,4},{4,5},{5,6},{6,7},{7,0},{8,9},{9,10},{10,1... | collective-permute-start | bytes 1990664 | tf_op jit(solution)/shard_map/ppermute | solution.py:30
  83.0 4.6 %collective-permute-start.2 = (f32[2,2,2,576,36]{3,2,4,1,0:T(2,128)S(1)}, f32[2,2,2,576,36]{3,2,4,1,0:T(2,128)}, u32[]{:S(2)}, u32[]{:S(2)}) collective-permute-start(f32[2,2,2,576,36]{3,2,4,1,0:T(2,128)S(1)} %collective-permute-done.1), channel_id=1, source_target_pairs={{0,7},{1,0},{2,1},{3,2},{4,3},{5,4},{6,5},{7,6},{8,15},{9,8},{10,9... | collective-permute-start | bytes 1990664 | tf_op jit(solution)/shard_map/ppermute | solution.py:33
  87.6 11.7 %collective-permute-done.5 = f32[2,2,2,576,36]{3,2,4,1,0:T(2,128)S(1)} collective-permute-done((f32[2,2,2,576,36]{3,2,4,1,0:T(2,128)S(1)}, f32[2,2,2,576,36]{3,2,4,1,0:T(2,128)S(1)}, u32[]{:S(2)}, u32[]{:S(2)}) %collective-permute-start.5) | collective-permute-done | bytes 663584 | tf_op jit(solution)/shard_map/ppermute | solution.py:30
  99.2 1.9 %collective-permute-start.6 = (f32[2,2,2,576,36]{3,2,4,1,0:T(2,128)S(1)}, f32[2,2,2,576,36]{3,2,4,1,0:T(2,128)}, u32[]{:S(2)}, u32[]{:S(2)}) collective-permute-start(f32[2,2,2,576,36]{3,2,4,1,0:T(2,128)S(1)} %collective-permute-done.5), channel_id=1, source_target_pairs={{0,1},{1,2},{2,3},{3,4},{4,5},{5,6},{6,7},{7,0},{8,9},{9,10},{10,1... | collective-permute-start | bytes 1990664 | tf_op jit(solution)/shard_map/ppermute | solution.py:30
  102.6 4.6 %collective-permute-start.3 = (f32[2,2,2,576,36]{3,2,4,1,0:T(2,128)}, f32[2,2,2,576,36]{3,2,4,1,0:T(2,128)S(1)}, u32[]{:S(2)}, u32[]{:S(2)}) collective-permute-start(f32[2,2,2,576,36]{3,2,4,1,0:T(2,128)} %collective-permute-done.2), channel_id=1, source_target_pairs={{0,7},{1,0},{2,1},{3,2},{4,3},{5,4},{6,5},{7,6},{8,15},{9,8},{10,9... | collective-permute-start | bytes 1990664 | tf_op jit(solution)/shard_map/ppermute | solution.py:33
  108.1 8.5 %collective-permute-done.6 = f32[2,2,2,576,36]{3,2,4,1,0:T(2,128)} collective-permute-done((f32[2,2,2,576,36]{3,2,4,1,0:T(2,128)S(1)}, f32[2,2,2,576,36]{3,2,4,1,0:T(2,128)}, u32[]{:S(2)}, u32[]{:S(2)}) %collective-permute-start.6) | collective-permute-done | bytes 663584 | tf_op jit(solution)/shard_map/ppermute | solution.py:30
  116.6 2.1 %collective-permute-start.7 = (f32[2,2,2,576,36]{3,2,4,1,0:T(2,128)}, f32[2,2,2,576,36]{3,2,4,1,0:T(2,128)S(1)}, u32[]{:S(2)}, u32[]{:S(2)}) collective-permute-start(f32[2,2,2,576,36]{3,2,4,1,0:T(2,128)} %collective-permute-done.6), channel_id=1, source_target_pairs={{0,1},{1,2},{2,3},{3,4},{4,5},{5,6},{6,7},{7,0},{8,9},{9,10},{10,1... | collective-permute-start | bytes 1990664 | tf_op jit(solution)/shard_map/ppermute | solution.py:30
  119.7 2.1 %bitcast_dynamic-update-slice_fusion.5 = f32[8,2,2,2,576,36]{4,5,1,0,2,3:T(8,128)} fusion(f32[8,2,2,2,576,36]{4,5,1,0,2,3:T(8,128)} %bitcast_dynamic-update-slice_fusion.6, f32[2,2,2,576,36]{3,2,4,1,0:T(2,128)} %collective-permute-done.2), kind=kLoop, calls=%fused_computation.15 | loop fusion | bytes 1556480
  122.7 10.5 %collective-permute-done.7 = f32[2,2,2,576,36]{3,2,4,1,0:T(2,128)S(1)} collective-permute-done((f32[2,2,2,576,36]{3,2,4,1,0:T(2,128)}, f32[2,2,2,576,36]{3,2,4,1,0:T(2,128)S(1)}, u32[]{:S(2)}, u32[]{:S(2)}) %collective-permute-start.7) | collective-permute-done | bytes 663584 | tf_op jit(solution)/shard_map/ppermute | solution.py:30
  134.2 2.1 %bitcast_dynamic-update-slice_fusion.2 = f32[8,2,2,2,576,36]{4,5,1,0,2,3:T(8,128)} fusion(f32[8,2,2,2,576,36]{4,5,1,0,2,3:T(8,128)} %bitcast_dynamic-update-slice_fusion.3, f32[2,2,2,576,36]{3,2,4,1,0:T(2,128)} %collective-permute-done.6), kind=kLoop, calls=%fused_computation.12 | loop fusion | bytes 1556480
  138.3 4.7 %all-gather.2.cloned.1.call-done = f32[2,576,2,576]{3,2,1,0:T(2,128)} async-done(((f32[2,36,2,576]{3,2,1,0:T(2,128)}), f32[2,576,2,576]{3,2,1,0:T(2,128)}) %all-gather.2.cloned.1.call-update) | async-done | bytes 5308432 | tf_op jit(solution)/shard_map/all_gather | solution.py:60
  143.0 3.3 %copy.34 = f32[2,2,8,36,2,576]{5,3,1,2,4,0:T(8,128)S(1)} copy(f32[2,2,8,36,2,576]{5,4,3,2,1,0:T(2,128)} %bitcast.53) | data formatting | bytes 10616832 | tf_op jit(solution)/shard_map/reshape | solution.py:62
  146.3 18.3 %fusion.2 = f32[2,576,2,576,1,1,1]{3,1,6,5,2,0,4:T(8,128)S(1)} fusion(s32[]{:T(128)S(6)} %select_n.21, f32[2,2,8,36,2,576]{5,3,1,2,4,0:T(8,128)S(1)} %copy.34, f32[8,2,2,2,576,36]{4,5,1,0,2,3:T(8,128)} %bitcast_dynamic-update-slice_fusion), kind=kOutput, calls=%fused_computation.4 | convolution fusion | flops 9174269952 | bytes 15925252 | tf_op jit(solution)/shard_map/yzikac,kzycjb->ijab/dot_general | solution.py:12
  165.0 8.9 %all_to_all.17 = f32[2,2,576,576]{2,3,1,0:T(8,128)S(1)} all-to-all(f32[2,2,576,576]{2,3,1,0:T(8,128)S(1)} %bitcast.52), channel_id=1, replica_groups=mesh['zh'=4,'x'=4,'core'=2,'zl'=2,'y'=8] {'core'}, dimensions={0} | all-to-all | bytes 10616832 | tf_op jit(solution)/shard_map/all_to_all | solution.py:66
  174.4 2.3 %copy.49 = f32[1,2,576,576]{3,2,1,0:T(8,128)} copy(f32[1,2,576,576]{2,3,1,0:T(8,128)S(1)} %fusion.5) | data formatting | bytes 5308416 | tf_op jit(solution)/shard_map/div | solution.py:76
  (32 shorter events, 14.0 us)
Async XLA Ops:
  6.5 36.3 %copy-start = (f32[4,18,2,576]{3,2,1,0:T(2,128)S(1)}, f32[4,18,2,576]{3,2,1,0:T(2,128)}, u32[]{:S(2)}) copy-start(f32[4,18,2,576]{3,2,1,0:T(2,128)} %param.5) | copy-start | bytes 995332
  6.5 136.5 %all-gather.2.cloned.1.call-start = ((), (), s32[]{:S(2)}) async-start(), calls=%async_computation.3 | async-start | bytes 6266880 | tf_op jit(solution)/shard_map/all_gather | solution.py:60
  42.6 58.5 %copy-start.2 = (f32[32]{0:T(128)S(1)}, f32[32]{0:T(128)}, u32[]{:S(2)}) copy-start(f32[32]{0:T(128)} %param.6) | copy-start | bytes 388
  42.6 59.9 %copy-start.1 = (f32[576]{0:T(1024)S(1)}, f32[576]{0:T(1024)}, u32[]{:S(2)}) copy-start(f32[576]{0:T(1024)} %param.7) | copy-start | bytes 6916
  47.9 12.9 %collective-permute-start = (f32[2,2,576,36]{2,3,0,1:T(8,128)S(1)}, f32[2,2,576,36]{2,3,0,1:T(8,128)S(1)}, u32[]{:S(2)}, u32[]{:S(2)}) collective-permute-start(f32[2,2,576,36]{2,3,0,1:T(8,128)S(1)} %copy.37), channel_id=1, source_target_pairs={{0,8},{8,0},{1,9},{9,1},{2,10},{10,2},{3,11},{11,3},{4,12},{12,4},... | collective-permute-start | bytes 995336 | tf_op jit(solution)/shard_map/ppermute | solution.py:53
  61.5 19.5 %collective-permute-start.4 = (f32[2,2,2,576,36]{3,2,4,1,0:T(2,128)S(1)}, f32[2,2,2,576,36]{3,2,4,1,0:T(2,128)S(1)}, u32[]{:S(2)}, u32[]{:S(2)}) collective-permute-start(f32[2,2,2,576,36]{3,2,4,1,0:T(2,128)S(1)} %copy.40), channel_id=1, source_target_pairs={{0,1},{1,2},{2,3},{3,4},{4,5},{5,6},{6,7},{7,0},{8,9},{9,10},{10,1... | collective-permute-start | bytes 1990664 | tf_op jit(solution)/shard_map/ppermute | solution.py:30
  64.7 18.2 %collective-permute-start.1 = (f32[2,2,2,576,36]{3,2,4,1,0:T(2,128)S(1)}, f32[2,2,2,576,36]{3,2,4,1,0:T(2,128)S(1)}, u32[]{:S(2)}, u32[]{:S(2)}) collective-permute-start(f32[2,2,2,576,36]{3,2,4,1,0:T(2,128)S(1)} %copy.40), channel_id=1, source_target_pairs={{0,7},{1,0},{2,1},{3,2},{4,3},{5,4},{6,5},{7,6},{8,15},{9,8},{10,9... | collective-permute-start | bytes 1990664 | tf_op jit(solution)/shard_map/ppermute | solution.py:33
  81.1 18.2 %collective-permute-start.5 = (f32[2,2,2,576,36]{3,2,4,1,0:T(2,128)S(1)}, f32[2,2,2,576,36]{3,2,4,1,0:T(2,128)S(1)}, u32[]{:S(2)}, u32[]{:S(2)}) collective-permute-start(f32[2,2,2,576,36]{3,2,4,1,0:T(2,128)S(1)} %collective-permute-done.4), channel_id=1, source_target_pairs={{0,1},{1,2},{2,3},{3,4},{4,5},{5,6},{6,7},{7,0},{8,9},{9,10},{10,1... | collective-permute-start | bytes 1990664 | tf_op jit(solution)/shard_map/ppermute | solution.py:30
  83.0 19.6 %collective-permute-start.2 = (f32[2,2,2,576,36]{3,2,4,1,0:T(2,128)S(1)}, f32[2,2,2,576,36]{3,2,4,1,0:T(2,128)}, u32[]{:S(2)}, u32[]{:S(2)}) collective-permute-start(f32[2,2,2,576,36]{3,2,4,1,0:T(2,128)S(1)} %collective-permute-done.1), channel_id=1, source_target_pairs={{0,7},{1,0},{2,1},{3,2},{4,3},{5,4},{6,5},{7,6},{8,15},{9,8},{10,9... | collective-permute-start | bytes 1990664 | tf_op jit(solution)/shard_map/ppermute | solution.py:33
  99.2 17.4 %collective-permute-start.6 = (f32[2,2,2,576,36]{3,2,4,1,0:T(2,128)S(1)}, f32[2,2,2,576,36]{3,2,4,1,0:T(2,128)}, u32[]{:S(2)}, u32[]{:S(2)}) collective-permute-start(f32[2,2,2,576,36]{3,2,4,1,0:T(2,128)S(1)} %collective-permute-done.5), channel_id=1, source_target_pairs={{0,1},{1,2},{2,3},{3,4},{4,5},{5,6},{6,7},{7,0},{8,9},{9,10},{10,1... | collective-permute-start | bytes 1990664 | tf_op jit(solution)/shard_map/ppermute | solution.py:30
  102.6 19.2 %collective-permute-start.3 = (f32[2,2,2,576,36]{3,2,4,1,0:T(2,128)}, f32[2,2,2,576,36]{3,2,4,1,0:T(2,128)S(1)}, u32[]{:S(2)}, u32[]{:S(2)}) collective-permute-start(f32[2,2,2,576,36]{3,2,4,1,0:T(2,128)} %collective-permute-done.2), channel_id=1, source_target_pairs={{0,7},{1,0},{2,1},{3,2},{4,3},{5,4},{6,5},{7,6},{8,15},{9,8},{10,9... | collective-permute-start | bytes 1990664 | tf_op jit(solution)/shard_map/ppermute | solution.py:33
  116.6 16.6 %collective-permute-start.7 = (f32[2,2,2,576,36]{3,2,4,1,0:T(2,128)}, f32[2,2,2,576,36]{3,2,4,1,0:T(2,128)S(1)}, u32[]{:S(2)}, u32[]{:S(2)}) collective-permute-start(f32[2,2,2,576,36]{3,2,4,1,0:T(2,128)} %collective-permute-done.6), channel_id=1, source_target_pairs={{0,1},{1,2},{2,3},{3,4},{4,5},{5,6},{6,7},{7,0},{8,9},{9,10},{10,1... | collective-permute-start | bytes 1990664 | tf_op jit(solution)/shard_map/ppermute | solution.py:30
Sparse Core Ops, SparseCore 0:
  47.5 95.5 all-gather.1
